TPU v7x, 128 devices: a whole 4x4x4 slice. The times are simulated.
128 devices in a mesh: row: 4 (over z), col: 32 (over x, y, core).
Axes of the slice: x: 4, y: 4, z: 4, core: 2. Of those that a mesh axis runs over, the one named last changes fastest.
Arguments:
- matrix_real: bfloat16 [512, 16384], P('col', 'row'), may hold values from -0.25 to 0.25
- matrix_imag: bfloat16 [512, 16384], P('col', 'row'), may hold values from -0.25 to 0.25
- valence_index: int32 [512], P('col'), may hold values from 0 to 15
- conduction_index: int32 [512], P('col'), may hold values from 0 to 31
- valence_energy: float32 [16], replicated, may hold values from -1.5 to -0.1
- conduction_energy: float32 [32], replicated, may hold values from 0.1 to 2
- frequency: float32 [2], replicated, may hold values from 0.2 to 2
Outputs:
- chi_real: bfloat16 [2, 16384, 16384], P(None, 'row', 'col')
- chi_imag: bfloat16 [2, 16384, 16384], P(None, 'row', 'col')
All inputs are finite; a program needn't handle non-finite values.
Results may differ from a plain program's by a relative error of at most 0.005.
Values may be sent and summed in bfloat16 or wider, within the bound.
No kernel may reach another device: no remote copies, remote signals or barrier semaphores. Data moves between devices by JAX's collectives and lax.ppermute only.
A program may use at most 192 MiB of HBM per device.

v0:
```python
import jax
import jax.numpy as jnp
from jax import lax
from jax.sharding import PartitionSpec as P


def lookup(indices, table):
    count = table.shape[0]
    picks = indices[:, None] == lax.broadcasted_iota(jnp.int32, (1, count), 1)
    return jnp.sum(jnp.where(picks, table[None, :], 0.0), axis=1)


def contract(left_side, right_side):
    return lax.dot_general(
        left_side, right_side, (((0,), (0,)), ((), ())), preferred_element_type=jnp.float32
    )


def on_device(
    matrix_real,
    matrix_imag,
    valence_index,
    conduction_index,
    valence_energy,
    conduction_energy,
    frequency,
):
    all_valence, all_conduction = (
        lax.all_gather(valence_index, "col", axis=0, tiled=True),
        lax.all_gather(conduction_index, "col", axis=0, tiled=True),
    )
    gap = lookup(all_conduction, conduction_energy) - lookup(all_valence, valence_energy)
    spread_real, spread_imag = (
        lax.all_gather(matrix_real, "row", axis=1, tiled=True),
        lax.all_gather(matrix_imag, "row", axis=1, tiled=True),
    )
    column_real, column_imag = (
        lax.all_to_all(spread_real, "col", split_axis=1, concat_axis=0, tiled=True),
        lax.all_to_all(spread_imag, "col", split_axis=1, concat_axis=0, tiled=True),
    )
    width = column_real.shape[1]
    wide_real = column_real.astype(jnp.float32)
    wide_imag = column_imag.astype(jnp.float32)
    upper_parts = []
    lower_parts = []
    for index in range(frequency.shape[0]):
        omega = frequency[index]
        weight = 4.0 * gap / (gap * gap + omega * omega)
        scaled_real = (weight[:, None] * wide_real).astype(jnp.bfloat16)
        scaled_imag = (weight[:, None] * wide_imag).astype(jnp.bfloat16)
        upper_parts.extend([scaled_real, scaled_imag])
        lower_parts.extend([scaled_imag, -scaled_real])
    upper_side = jnp.concatenate(upper_parts, axis=1)
    lower_side = jnp.concatenate(lower_parts, axis=1)
    right_side = jnp.concatenate([upper_side, lower_side], axis=0)
    block_real, block_imag = (
        lax.all_to_all(matrix_real, "col", split_axis=1, concat_axis=0, tiled=True),
        lax.all_to_all(matrix_imag, "col", split_axis=1, concat_axis=0, tiled=True),
    )
    stacked = jnp.concatenate([block_real, block_imag], axis=0)
    joined = contract(lax.all_gather(stacked, "col", axis=1, tiled=True), right_side)
    real_out = []
    imag_out = []
    for index in range(frequency.shape[0]):
        start = 2 * width * index
        real_out.append((-joined[:, start : start + width]).astype(jnp.bfloat16))
        imag_out.append((-joined[:, start + width : start + 2 * width]).astype(jnp.bfloat16))
    return (jnp.stack(real_out, axis=0), jnp.stack(imag_out, axis=0))


def solution(mesh):
    placed = (P("col", "row"), P("col", "row"), P("col"), P("col"), P(), P(), P())
    return jax.shard_map(
        on_device,
        mesh=mesh,
        in_specs=placed,
        out_specs=(P(None, "row", "col"), P(None, "row", "col")),
        check_vma=False,
    )
```

profile of v0, /device:TPU:1, one launch (start us, length us, event | category | flops | bytes accessed | tf_op | source)
XLA Modules:
  0.0 199.1 jit_solution(13468990475961677798)
XLA Ops:
  7.2 1.6 copy_bitcast_fusion.3
  8.7 8.6 %all-to-all-start = ((bf16[16,32,128]{2,0,1:T(8,128)(2,1)}), bf16[16,32,128]{2,0,1:T(8,128)(2,1)S(1)}, u32[]{:S(2)}, u32[]{:S(2)}) async-start(bf16[16,32,128]{2,0,1:T(8,128)(2,1)} %copy_bitcast_fusion.3), calls=%async_computation | async-start | bytes 262144 | tf_op jit(solution)/shard_map/all_to_all | solution.py:57
  17.3 0.0 all-gather.2.cloned.1.call-start
  17.4 0.9 copy_bitcast_fusion.2
  18.3 6.7 %all-to-all-done = bf16[16,32,128]{2,0,1:T(8,128)(2,1)S(1)} async-done(((bf16[16,32,128]{2,0,1:T(8,128)(2,1)}), bf16[16,32,128]{2,0,1:T(8,128)(2,1)S(1)}, u32[]{:S(2)}, u32[]{:S(2)}) %all-to-all-start) | async-done | bytes 131104 | tf_op jit(solution)/shard_map/all_to_all | solution.py:57
  25.0 11.3 %all_to_all.64 = bf16[16,32,128]{2,0,1:T(8,128)(2,1)S(1)} all-to-all(bf16[16,32,128]{2,0,1:T(8,128)(2,1)S(1)} %copy_bitcast_fusion.2), channel_id=1, replica_groups=mesh['row'=4,'col'=32] {'col'}, dimensions={1} | all-to-all | bytes 262144 | tf_op jit(solution)/shard_map/all_to_all | solution.py:58
  36.3 0.7 pad_maximum_fusion.2
  37.0 0.0 all-gather.2.cloned.1.call-update
  37.1 12.7 %all_gather.19 = bf16[16,16384]{1,0:T(8,128)(2,1)S(1)} all-gather(bf16[16,4096]{1,0:T(8,128)(2,1)} %param.8), channel_id=1, replica_groups=mesh['row'=4,'col'=32] {'row'}, dimensions={1}, use_global_device_ids=true | all-gather | bytes 655360 | tf_op jit(solution)/shard_map/all_gather | solution.py:35
  49.7 0.9 copy.29
  50.6 5.5 %all-to-all-start.3 = ((bf16[16,32,512]{2,0,1:T(8,128)(2,1)}), bf16[16,32,512]{2,0,1:T(8,128)(2,1)S(1)}, u32[]{:S(2)}, u32[]{:S(2)}) async-start(bf16[16,32,512]{2,0,1:T(8,128)(2,1)} %bitcast.54), calls=%async_computation.3 | async-start | bytes 1048576 | tf_op jit(solution)/shard_map/all_to_all | solution.py:39
  56.1 12.0 %all_gather.18 = bf16[16,16384]{1,0:T(8,128)(2,1)S(1)} all-gather(bf16[16,4096]{1,0:T(8,128)(2,1)} %param.7), channel_id=1, replica_groups=mesh['row'=4,'col'=32] {'row'}, dimensions={1}, use_global_device_ids=true | all-gather | bytes 655360 | tf_op jit(solution)/shard_map/all_gather | solution.py:34
  68.1 0.9 copy.30
  68.9 1.3 dynamic-slice
  70.8 0.9 dynamic-update-slice
  71.7 0.9 dynamic-update-slice.1
  72.5 15.7 %all-reduce.2 = (s32[512]{0:T(512)S(1)}, s32[512]{0:T(512)S(1)}) all-reduce(s32[512]{0:T(512)S(1)} %dynamic-update-slice, s32[512]{0:T(512)S(1)} %dynamic-update-slice.1), channel_id=1, replica_groups=mesh['row'=4,'col'=32] {'col'}, use_global_device_ids=true, to_apply=%add | all-reduce | flops 1024 | bytes 8192
  88.3 0.7 select_reduce_fusion.1
  89.0 0.7 select_reduce_fusion
  89.8 0.0 all-to-all-done.3
  89.8 6.8 %all-to-all-start.2 = ((bf16[16,32,512]{2,0,1:T(8,128)(2,1)}), bf16[16,32,512]{2,0,1:T(8,128)(2,1)S(1)}, u32[]{:S(2)}, u32[]{:S(2)}) async-start(bf16[16,32,512]{2,0,1:T(8,128)(2,1)} %bitcast.55), calls=%async_computation.2 | async-start | bytes 1048576 | tf_op jit(solution)/shard_map/all_to_all | solution.py:38
  96.6 1.3 fusion.33
  100.5 0.2 fusion.24
  100.7 7.6 %all-to-all-done.2 = bf16[16,32,512]{2,0,1:T(8,128)(2,1)S(1)} async-done(((bf16[16,32,512]{2,0,1:T(8,128)(2,1)}), bf16[16,32,512]{2,0,1:T(8,128)(2,1)S(1)}, u32[]{:S(2)}, u32[]{:S(2)}) %all-to-all-start.2) | async-done | bytes 524320 | tf_op jit(solution)/shard_map/all_to_all | solution.py:38
  108.3 1.1 fusion.29
  109.4 0.0 all-gather.2.cloned.1.call-done
  109.4 52.4 %fusion.8 = f32[4096,2048]{1,0:T(8,128)} fusion(bf16[1024,4096]{1,0:T(8,128)(2,1)} %all-gather.2.cloned.1.call-done, bf16[512,512]{1,0:T(8,128)(2,1)S(1)} %get-tuple-element.14, bf16[512,512]{1,0:T(8,128)(2,1)S(1)} %get-tuple-element.13, bf16[512,512]{1,0:T(8,128)(2,1)S(1)} %get-tuple-element.4, bf16[512,512]{1,0:T(8,128)(2,1)S(1)} %get-tuple-element.12, ...), kind=kOutput, calls=%fused_computation.14 | convolution fusion | flops 17213423616 | bytes 45088768 | tf_op jit(solution)/shard_map/dot_general | solution.py:14
  161.8 18.9 %fusion.6 = (bf16[1,4096,512]{2,1,0:T(8,128)(2,1)}, bf16[1,4096,512]{2,1,0:T(8,128)(2,1)}, bf16[1,4096,512]{2,1,0:T(8,128)(2,1)}, bf16[1,4096,512]{2,1,0:T(8,128)(2,1)}) fusion(f32[4096,2048]{1,0:T(8,128)} %fusion.8), kind=kLoop, calls=%fused_computation.12 | loop fusion | flops 16777216 | bytes 50331648 | tf_op jit(solution)/shard_map/stack | solution.py:68
  180.7 11.5 %pad_maximum_fusion = (bf16[2,4096,512]{2,1,0:T(8,128)(2,1)}, bf16[2,4096,512]{2,1,0:T(8,128)(2,1)}) fusion(bf16[1,4096,512]{2,1,0:T(8,128)(2,1)} %get-tuple-element.10, bf16[1,4096,512]{2,1,0:T(8,128)(2,1)} %get-tuple-element.11, bf16[1,4096,512]{2,1,0:T(8,128)(2,1)} %get-tuple-element.9, bf16[1,4096,512]{2,1,0:T(8,128)(2,1)} %get-tuple-element.8), kind=kLoop, calls=%fused_computation.8 | loop fusion | flops 8388608 | bytes 33554432 | tf_op jit(solution)/shard_map/stack | solution.py:68
  (3 shorter events, 0.0 us)
Async XLA Ops:
  8.7 16.3 %all-to-all-start = ((bf16[16,32,128]{2,0,1:T(8,128)(2,1)}), bf16[16,32,128]{2,0,1:T(8,128)(2,1)S(1)}, u32[]{:S(2)}, u32[]{:S(2)}) async-start(bf16[16,32,128]{2,0,1:T(8,128)(2,1)} %copy_bitcast_fusion.3), calls=%async_computation | async-start | bytes 262144 | tf_op jit(solution)/shard_map/all_to_all | solution.py:57
  17.3 92.1 %all-gather.2.cloned.1.call-start = ((), (), s32[]{:S(2)}) async-start(), calls=%async_computation.4 | async-start | bytes 8650752 | tf_op jit(solution)/shard_map/all_gather | solution.py:61
  50.6 39.2 %all-to-all-start.3 = ((bf16[16,32,512]{2,0,1:T(8,128)(2,1)}), bf16[16,32,512]{2,0,1:T(8,128)(2,1)S(1)}, u32[]{:S(2)}, u32[]{:S(2)}) async-start(bf16[16,32,512]{2,0,1:T(8,128)(2,1)} %bitcast.54), calls=%async_computation.3 | async-start | bytes 1048576 | tf_op jit(solution)/shard_map/all_to_all | solution.py:39
  89.8 18.5 %all-to-all-start.2 = ((bf16[16,32,512]{2,0,1:T(8,128)(2,1)}), bf16[16,32,512]{2,0,1:T(8,128)(2,1)S(1)}, u32[]{:S(2)}, u32[]{:S(2)}) async-start(bf16[16,32,512]{2,0,1:T(8,128)(2,1)} %bitcast.55), calls=%async_computation.2 | async-start | bytes 1048576 | tf_op jit(solution)/shard_map/all_to_all | solution.py:38
Sparse Core Ops, SparseCore 0:
  37.2 62.9 all-gather.1
where the time goes:
time: 200 us; the launch traced here: 199 us
  matrix products  52.4 us (26%)
  blocking collectives  51.7 us (26%)
  other arithmetic  34 us (17%)
  starting transfers between devices  20.9 us (10%)
  between operations  17.3 us (9%)
  waiting for transfers between devices  14.3 us (7%)
  local copies, waits for them, and re-layouts  8.55 us (4%)
    dot_general x1, matrix products, contract(): lax.dot_general(left_side, right_side, (((0,), (0,)), ((), ())), preferre...  52.4 us
    another operation x2, other arithmetic, on_device(): return (jnp.stack(real_out, axis=0), jnp.stack(imag_out, axis=0))  30.5 us
    unnamed x1, blocking collectives  15.7 us
    all_gather x1, blocking collectives, on_device(): lax.all_gather(matrix_imag, 'row', axis=1, tiled=True)  12.7 us
    all_gather x1, blocking collectives, on_device(): lax.all_gather(matrix_real, 'row', axis=1, tiled=True)  12 us
    all_to_all x1, blocking collectives, on_device(): lax.all_to_all(matrix_imag, 'col', split_axis=1, concat_axis=0, tiled=True)  11.3 us
    all_to_all x1, starting transfers between devices, on_device(): lax.all_to_all(matrix_real, 'col', split_axis=1, concat_axis=0, tiled=True)  8.59 us
    all_to_all x1, waiting for transfers between devices, on_device(): lax.all_to_all(spread_real, 'col', split_axis=1, concat_axis=0, tiled=True)  7.6 us
  transfers between devices with their start and end apart: 4, of which 2 were waited for; matrix products, arithmetic and copies ran while one was open for 5% of the time, Pallas kernels for 0%

commit v1 on v0

--- a/solution.py
+++ b/solution.py
@@ -2,6 +2,35 @@
 import jax.numpy as jnp
 from jax import lax
 from jax.sharding import PartitionSpec as P
+from jax.lax import axis_index, axis_size, ppermute
+
+
+def wait_unit(array_here, row_dim):
+    res = list(array_here.shape[1:])
+    res[row_dim] *= array_here.shape[0]
+    v1 = jnp.moveaxis(array_here, 0, row_dim).reshape(res)
+    return v1
+
+
+def proceed_numbers(buf, axis_tag, out_dim):
+    tray = []
+    total_devices = axis_size(axis_tag)
+    for dd in range(total_devices):
+        tray.append((dd, (dd + 1) % total_devices))
+    parts_seen = []
+    for j, no in tray:
+        parts_seen.append((no, j))
+    w_next, q_next = ([], [])
+    for to_i in range(total_devices - 1):
+        if to_i % 2 == 0:
+            w_next.append(ppermute(w_next[-1] if w_next else buf, axis_tag, tray))
+        else:
+            q_next.append(ppermute(q_next[-1] if q_next else buf, axis_tag, parts_seen))
+    top = jnp.stack([*w_next[::-1], buf, *q_next], axis=0)
+    lower = axis_index(axis_tag) - len(w_next)
+    top = top[(jnp.arange(total_devices) - lower) % total_devices]
+    raw_out = wait_unit(top, out_dim)
+    return raw_out
 
 
 def lookup(indices, table):
@@ -31,7 +60,7 @@
     )
     gap = lookup(all_conduction, conduction_energy) - lookup(all_valence, valence_energy)
     spread_real, spread_imag = (
-        lax.all_gather(matrix_real, "row", axis=1, tiled=True),
+        proceed_numbers(matrix_real, "row", 1),
         lax.all_gather(matrix_imag, "row", axis=1, tiled=True),
     )
     column_real, column_imag = (

time: 200 us -> 198 us (0.990)
  blocking collectives: 51.7 us -> 36.5 us
  starting transfers between devices: 20.9 us -> 27.3 us
  waiting for transfers between devices: 14.3 us -> 19.7 us
    all_gather x1 -> x0, blocking collectives: 12 us -> none  [on_device(): lax.all_gather(matrix_real, 'row', axis=1, tiled=True)]
    ppermute x0 -> x3, starting transfers between devices: none -> 4.87 us  [the longest x2 2.67 us: proceed_numbers(): w_next.append(ppermute(w_next[-1] if w_next else buf, axis_tag, tray))]
    ppermute x0 -> x3, waiting for transfers between devices: none -> 4.51 us  [the longest x2 4.5 us: proceed_numbers(): w_next.append(ppermute(w_next[-1] if w_next else buf, axis_tag, tray))]
  transfers between devices with their start and end apart: 4 -> 7, of which waited for: 2 -> 3; matrix products, arithmetic and copies ran while one was open for 5% -> 6% of each run, Pallas kernels for 0% -> 0%
where the time goes in v1:
time: 198 us; the launch traced here: 197 us
  matrix products  52.4 us (26%)
  blocking collectives  36.5 us (18%)
  other arithmetic  35 us (18%)
  starting transfers between devices  27.3 us (14%)
  waiting for transfers between devices  19.7 us (10%)
  between operations  17.2 us (9%)
  local copies, waits for them, and re-layouts  9.36 us (5%)
    dot_general x1, matrix products, contract(): lax.dot_general(left_side, right_side, (((0,), (0,)), ((), ())), preferre...  52.4 us
    another operation x2, other arithmetic, on_device(): return (jnp.stack(real_out, axis=0), jnp.stack(imag_out, axis=0))  30.5 us
    unnamed x1, blocking collectives  14.2 us
    all_to_all x1, blocking collectives, on_device(): lax.all_to_all(matrix_real, 'col', split_axis=1, concat_axis=0, tiled=True)  11.3 us
    all_gather x1, blocking collectives, on_device(): lax.all_gather(matrix_imag, 'row', axis=1, tiled=True)  11 us
    all_to_all x1, starting transfers between devices, on_device(): lax.all_to_all(matrix_imag, 'col', split_axis=1, concat_axis=0, tiled=True)  8.59 us
    all_to_all x1, waiting for transfers between devices, on_device(): lax.all_to_all(spread_real, 'col', split_axis=1, concat_axis=0, tiled=True)  8.47 us
    all_to_all x1, starting transfers between devices, on_device(): lax.all_to_all(spread_real, 'col', split_axis=1, concat_axis=0, tiled=True)  7.23 us
  transfers between devices with their start and end apart: 7, of which 3 were waited for; matrix products, arithmetic and copies ran while one was open for 6% of the time, Pallas kernels for 0%

profile of v1, /device:TPU:1, one launch (start us, length us, event | category | flops | bytes accessed | tf_op | source)
XLA Modules:
  0.0 197.5 jit_solution(8751221792656040309)
XLA Ops:
  7.2 0.0 copy-start
  7.2 1.6 copy_bitcast_fusion.1
  8.8 8.6 %all-to-all-start.1 = ((bf16[16,32,128]{2,0,1:T(8,128)(2,1)}), bf16[16,32,128]{2,0,1:T(8,128)(2,1)S(1)}, u32[]{:S(2)}, u32[]{:S(2)}) async-start(bf16[16,32,128]{2,0,1:T(8,128)(2,1)} %copy_bitcast_fusion.1), calls=%async_computation.1 | async-start | bytes 262144 | tf_op jit(solution)/shard_map/all_to_all | solution.py:87
  17.4 0.0 all-gather.2.cloned.1.call-start
  17.4 0.9 copy_bitcast_fusion.2
  18.3 6.7 %all-to-all-done.1 = bf16[16,32,128]{2,0,1:T(8,128)(2,1)S(1)} async-done(((bf16[16,32,128]{2,0,1:T(8,128)(2,1)}), bf16[16,32,128]{2,0,1:T(8,128)(2,1)S(1)}, u32[]{:S(2)}, u32[]{:S(2)}) %all-to-all-start.1) | async-done | bytes 131104 | tf_op jit(solution)/shard_map/all_to_all | solution.py:87
  25.1 11.3 %all_to_all.64 = bf16[16,32,128]{2,0,1:T(8,128)(2,1)S(1)} all-to-all(bf16[16,32,128]{2,0,1:T(8,128)(2,1)S(1)} %copy_bitcast_fusion.2), channel_id=1, replica_groups=mesh['row'=4,'col'=32] {'col'}, dimensions={1} | all-to-all | bytes 262144 | tf_op jit(solution)/shard_map/all_to_all | solution.py:86
  36.3 0.7 pad_maximum_fusion.3
  37.1 0.0 all-gather.2.cloned.1.call-update
  37.1 1.7 collective-permute-start
  38.8 2.2 %collective-permute-start.2 = (bf16[16,4096]{1,0:T(8,128)(2,1)}, bf16[16,4096]{1,0:T(8,128)(2,1)S(1)}, u32[]{:S(2)}, u32[]{:S(2)}) collective-permute-start(bf16[16,4096]{1,0:T(8,128)(2,1)} %param.7), channel_id=1, source_target_pairs={{32,0},{64,32},{96,64},{0,96},{33,1},{65,33},{97,65},{1,97},{34,2}... | collective-permute-start | bytes 393224 | tf_op jit(solution)/shard_map/ppermute | solution.py:28
  41.0 11.0 %all_gather.15 = bf16[16,16384]{1,0:T(8,128)(2,1)S(1)} all-gather(bf16[16,4096]{1,0:T(8,128)(2,1)} %param.8), channel_id=1, replica_groups=mesh['row'=4,'col'=32] {'row'}, dimensions={1}, use_global_device_ids=true | all-gather | bytes 655360 | tf_op jit(solution)/shard_map/all_gather | solution.py:64
  52.0 0.9 copy.31
  52.8 6.6 %all-to-all-start.3 = ((bf16[16,32,512]{2,0,1:T(8,128)(2,1)}), bf16[16,32,512]{2,0,1:T(8,128)(2,1)S(1)}, u32[]{:S(2)}, u32[]{:S(2)}) async-start(bf16[16,32,512]{2,0,1:T(8,128)(2,1)} %bitcast.58), calls=%async_computation.3 | async-start | bytes 1048576 | tf_op jit(solution)/shard_map/all_to_all | solution.py:68
  59.4 1.2 dynamic-slice
  61.3 0.9 dynamic-update-slice
  62.2 0.8 dynamic-update-slice.1
  63.0 14.2 %all-reduce.2 = (s32[512]{0:T(512)S(1)}, s32[512]{0:T(512)S(1)}) all-reduce(s32[512]{0:T(512)S(1)} %dynamic-update-slice, s32[512]{0:T(512)S(1)} %dynamic-update-slice.1), channel_id=1, replica_groups=mesh['row'=4,'col'=32] {'col'}, use_global_device_ids=true, to_apply=%add | all-reduce | flops 1024 | bytes 8192
  77.3 0.8 select_reduce_fusion.1
  78.0 0.7 select_reduce_fusion
  78.8 0.0 collective-permute-done
  78.8 1.0 collective-permute-start.1
  79.8 0.0 collective-permute-done.2
  79.8 4.5 %collective-permute-done.1 = bf16[16,4096]{1,0:T(8,128)(2,1)S(1)} collective-permute-done((bf16[16,4096]{1,0:T(8,128)(2,1)S(1)}, bf16[16,4096]{1,0:T(8,128)(2,1)S(1)}, u32[]{:S(2)}, u32[]{:S(2)}) %collective-permute-start.1) | collective-permute-done | bytes 131104 | tf_op jit(solution)/shard_map/ppermute | solution.py:26
  84.3 1.0 pad_maximum_fusion.2
  85.3 0.6 gather_fusion
  85.8 0.4 copy.22
  86.3 0.4 all_to_all.56
  86.6 1.1 copy.23
  87.7 0.0 all-to-all-done.3
  87.7 7.2 %all-to-all-start.2 = ((bf16[16,32,512]{2,0,1:T(8,128)(2,1)}), bf16[16,32,512]{2,0,1:T(8,128)(2,1)S(1)}, u32[]{:S(2)}, u32[]{:S(2)}) async-start(bf16[16,32,512]{2,0,1:T(8,128)(2,1)} %copy.23), calls=%async_computation.2 | async-start | bytes 1048576 | tf_op jit(solution)/shard_map/all_to_all | solution.py:67
  95.0 0.0 copy-done
  95.0 0.6 fusion.35
  98.0 0.2 fusion.24
  98.2 8.5 %all-to-all-done.2 = bf16[16,32,512]{2,0,1:T(8,128)(2,1)S(1)} async-done(((bf16[16,32,512]{2,0,1:T(8,128)(2,1)}), bf16[16,32,512]{2,0,1:T(8,128)(2,1)S(1)}, u32[]{:S(2)}, u32[]{:S(2)}) %all-to-all-start.2) | async-done | bytes 524320 | tf_op jit(solution)/shard_map/all_to_all | solution.py:67
  106.7 1.1 fusion.31
  107.8 0.0 all-gather.2.cloned.1.call-done
  107.8 52.4 %fusion.8 = f32[4096,2048]{1,0:T(8,128)} fusion(bf16[1024,4096]{1,0:T(8,128)(2,1)} %all-gather.2.cloned.1.call-done, bf16[512,512]{1,0:T(8,128)(2,1)S(1)} %get-tuple-element.14, bf16[512,512]{1,0:T(8,128)(2,1)S(1)} %get-tuple-element.13, bf16[512,512]{1,0:T(8,128)(2,1)S(1)} %get-tuple-element.4, bf16[512,512]{1,0:T(8,128)(2,1)S(1)} %get-tuple-element.12, ...), kind=kOutput, calls=%fused_computation.15 | convolution fusion | flops 17213423616 | bytes 45088768 | tf_op jit(solution)/shard_map/dot_general | solution.py:43
  160.2 18.9 %fusion.6 = (bf16[1,4096,512]{2,1,0:T(8,128)(2,1)}, bf16[1,4096,512]{2,1,0:T(8,128)(2,1)}, bf16[1,4096,512]{2,1,0:T(8,128)(2,1)}, bf16[1,4096,512]{2,1,0:T(8,128)(2,1)}) fusion(f32[4096,2048]{1,0:T(8,128)} %fusion.8), kind=kLoop, calls=%fused_computation.13 | loop fusion | flops 16777216 | bytes 50331648 | tf_op jit(solution)/shard_map/stack | solution.py:97
  179.1 11.5 %pad_maximum_fusion = (bf16[2,4096,512]{2,1,0:T(8,128)(2,1)}, bf16[2,4096,512]{2,1,0:T(8,128)(2,1)}) fusion(bf16[1,4096,512]{2,1,0:T(8,128)(2,1)} %get-tuple-element.10, bf16[1,4096,512]{2,1,0:T(8,128)(2,1)} %get-tuple-element.11, bf16[1,4096,512]{2,1,0:T(8,128)(2,1)} %get-tuple-element.9, bf16[1,4096,512]{2,1,0:T(8,128)(2,1)} %get-tuple-element.8), kind=kLoop, calls=%fused_computation.9 | loop fusion | flops 8388608 | bytes 33554432 | tf_op jit(solution)/shard_map/stack | solution.py:97
  (5 shorter events, 0.0 us)
Async XLA Ops:
  7.2 87.8 %copy-start = (f32[2]{0:T(128)S(1)}, f32[2]{0:T(128)}, u32[]{:S(2)}) copy-start(f32[2]{0:T(128)} %param.13) | copy-start | bytes 28
  8.8 16.3 %all-to-all-start.1 = ((bf16[16,32,128]{2,0,1:T(8,128)(2,1)}), bf16[16,32,128]{2,0,1:T(8,128)(2,1)S(1)}, u32[]{:S(2)}, u32[]{:S(2)}) async-start(bf16[16,32,128]{2,0,1:T(8,128)(2,1)} %copy_bitcast_fusion.1), calls=%async_computation.1 | async-start | bytes 262144 | tf_op jit(solution)/shard_map/all_to_all | solution.py:87
  17.4 90.5 %all-gather.2.cloned.1.call-start = ((), (), s32[]{:S(2)}) async-start(), calls=%async_computation.4 | async-start | bytes 8650752 | tf_op jit(solution)/shard_map/all_gather | solution.py:90
  37.1 41.7 %collective-permute-start = (bf16[16,4096]{1,0:T(8,128)(2,1)}, bf16[16,4096]{1,0:T(8,128)(2,1)S(1)}, u32[]{:S(2)}, u32[]{:S(2)}) collective-permute-start(bf16[16,4096]{1,0:T(8,128)(2,1)} %param.7), channel_id=1, source_target_pairs={{0,32},{32,64},{64,96},{96,0},{1,33},{33,65},{65,97},{97,1},{2,34}... | collective-permute-start | bytes 393224 | tf_op jit(solution)/shard_map/ppermute | solution.py:26
  38.8 41.0 %collective-permute-start.2 = (bf16[16,4096]{1,0:T(8,128)(2,1)}, bf16[16,4096]{1,0:T(8,128)(2,1)S(1)}, u32[]{:S(2)}, u32[]{:S(2)}) collective-permute-start(bf16[16,4096]{1,0:T(8,128)(2,1)} %param.7), channel_id=1, source_target_pairs={{32,0},{64,32},{96,64},{0,96},{33,1},{65,33},{97,65},{1,97},{34,2}... | collective-permute-start | bytes 393224 | tf_op jit(solution)/shard_map/ppermute | solution.py:28
  52.8 34.9 %all-to-all-start.3 = ((bf16[16,32,512]{2,0,1:T(8,128)(2,1)}), bf16[16,32,512]{2,0,1:T(8,128)(2,1)S(1)}, u32[]{:S(2)}, u32[]{:S(2)}) async-start(bf16[16,32,512]{2,0,1:T(8,128)(2,1)} %bitcast.58), calls=%async_computation.3 | async-start | bytes 1048576 | tf_op jit(solution)/shard_map/all_to_all | solution.py:68
  78.8 5.5 %collective-permute-start.1 = (bf16[16,4096]{1,0:T(8,128)(2,1)S(1)}, bf16[16,4096]{1,0:T(8,128)(2,1)S(1)}, u32[]{:S(2)}, u32[]{:S(2)}) collective-permute-start(bf16[16,4096]{1,0:T(8,128)(2,1)S(1)} %collective-permute-done), channel_id=1, source_target_pairs={{0,32},{32,64},{64,96},{96,0},{1,33},{33,65},{65,97},{97,1},{2,34}... | collective-permute-start | bytes 393224 | tf_op jit(solution)/shard_map/ppermute | solution.py:26
  87.7 19.0 %all-to-all-start.2 = ((bf16[16,32,512]{2,0,1:T(8,128)(2,1)}), bf16[16,32,512]{2,0,1:T(8,128)(2,1)S(1)}, u32[]{:S(2)}, u32[]{:S(2)}) async-start(bf16[16,32,512]{2,0,1:T(8,128)(2,1)} %copy.23), calls=%async_computation.2 | async-start | bytes 1048576 | tf_op jit(solution)/shard_map/all_to_all | solution.py:67
Sparse Core Ops, SparseCore 0:
  37.2 58.3 all-gather.1
